TPU v7x, 256 devices: a whole 4x4x8 slice. The times are simulated.
256 devices in a mesh: dp: 32 (over x, z), own: 8 (over y, core).
Axes of the slice: x: 4, y: 4, z: 8, core: 2. Of those that a mesh axis runs over, the one named last changes fastest.
Arguments:
- partials: bfloat16 [32, 64, 256, 1024], P('dp', None, None, 'own')
- owner: int32 [64, 1], replicated, may hold values from 0 to 31; in each aligned block of 64 rows (0 to 63, 64 to 127, ...) at most 4 rows name the same one
- momentum: float32 [32, 4, 256, 1024], P('dp', None, None, 'own'), may hold values from -1.2 to 1.2
- master: float32 [32, 4, 256, 1024], P('dp', None, None, 'own'), may hold values from -0.3 to 0.3
Outputs:
- new_momentum: float32 [32, 4, 256, 1024], P('dp', None, None, 'own')
- new_master: float32 [32, 4, 256, 1024], P('dp', None, None, 'own')
- new_weights: bfloat16 [64, 256, 1024], P(None, None, 'own')
Inputs may be any that keep to these rules, and one draw needn't show every extreme that they name: `owner`: every group owns at least one block and at most 4 blocks; some group owns exactly 4.
All inputs are finite; a program needn't handle non-finite values.
Results may differ from a plain program's by a relative error of at most 0.0007.
Values may be sent and summed in bfloat16 or wider, within the bound.
No kernel may reach another device: no remote copies, remote signals or barrier semaphores. Data moves between devices by JAX's collectives and lax.ppermute only.
A program may use at most 128 MiB of HBM per device.

v0:
```python
import math
import jax
import jax.numpy as jnp
from jax import lax
from jax.sharding import PartitionSpec as P

D = 1024
ITERS = 5
COEF_A = 3.4445
COEF_B = -4.775
COEF_C = 2.0315
BETA = 0.95
STEP_SIZE = 0.2
DECAY = 0.1
EPSILON = 1e-07


def slot_targets(owner_list, group_count, slot_count):
    onehot = (owner_list[:, None] == jnp.arange(group_count, dtype=jnp.int32)[None, :]).astype(
        jnp.int32
    )
    before = jnp.cumsum(onehot, axis=0) - onehot
    ranks = jnp.sum(before * onehot, axis=1)
    return owner_list * slot_count + ranks


def slot_sources(target, slot_count, block_count):
    positions = jnp.arange(slot_count, dtype=jnp.int32)
    matches = positions[:, None] == target[None, :]
    present = jnp.any(matches, axis=1)
    source = jnp.sum(
        jnp.where(matches, jnp.arange(block_count, dtype=jnp.int32)[None, :], 0), axis=1
    )
    return (present, source)


def local_gram(values):
    return jnp.einsum(
        "srk,stk->srt",
        values,
        values,
        precision=lax.Precision.HIGHEST,
        preferred_element_type=jnp.float32,
    )


def gram_total(values):
    return lax.psum(local_gram(values), "own")


def newton_turn(ortho, gram):
    square = jnp.einsum(
        "srt,stu->sru",
        gram,
        gram,
        precision=lax.Precision.HIGHEST,
        preferred_element_type=jnp.float32,
    )
    poly = COEF_B * gram + COEF_C * square
    product = jnp.einsum(
        "srt,stk->srk",
        poly,
        ortho,
        precision=lax.Precision.HIGHEST,
        preferred_element_type=jnp.float32,
    )
    return COEF_A * ortho + product


def on_device(partials, owner, momentum, master):
    group_count = lax.axis_size("dp")
    local_rows = partials[0]
    block_count = local_rows.shape[0]
    slot_count = momentum.shape[1]
    block_rows = momentum.shape[2]
    owner_list = owner[:, 0]
    target = slot_targets(owner_list, group_count, slot_count)
    present, source = slot_sources(target, group_count * slot_count, block_count)
    outgoing = jnp.where(
        present[:, None, None], jnp.take(local_rows, source, axis=0).astype(jnp.float32), 0.0
    )
    gradient = lax.psum_scatter(outgoing, "dp", scatter_dimension=0, tiled=True)
    momentum_new = BETA * momentum[0] + gradient
    update = gradient + BETA * momentum_new
    squares = lax.psum(jnp.sum(update * update, axis=(1, 2)), "own")
    factor = 1.0 / (jnp.sqrt(squares) + EPSILON)
    ortho = update * factor[:, None, None]
    gram = gram_total(ortho)
    for iteration in range(ITERS):
        if iteration > 0:
            gram = gram_total(ortho)
        ortho = newton_turn(ortho, gram)
    step_factor = STEP_SIZE * 0.2 * math.sqrt(max(block_rows, D))
    master_new = master[0] * (1.0 - STEP_SIZE * DECAY) - step_factor * ortho
    weights_low = master_new.astype(jnp.bfloat16)
    every_slot = lax.all_gather(weights_low, "dp", axis=0, tiled=True)
    weights = jnp.take(every_slot, target, axis=0)
    return (momentum_new[None], master_new[None], weights)


def solution(mesh):
    in_specs = (
        P("dp", None, None, "own"),
        P(),
        P("dp", None, None, "own"),
        P("dp", None, None, "own"),
    )
    out_specs = (P("dp", None, None, "own"), P("dp", None, None, "own"), P(None, None, "own"))
    return jax.shard_map(
        on_device, mesh=mesh, in_specs=in_specs, out_specs=out_specs, check_vma=False
    )
```

profile of v0, /device:TPU:1, one launch (start us, length us, event | category | flops | bytes accessed | tf_op | source)
XLA Modules:
  0.0 780.1 jit_solution(16891098648073873890)
XLA Ops:
  7.2 0.0 reduce-scatter.2.cloned.1.call-start
  7.2 0.7 fusion.13
  7.9 0.1 reduce_window_sum.11
  8.0 0.8 select_reduce_fusion.1
  8.9 0.7 multiply_add_fusion.1
  9.5 0.1 select_reduce_fusion
  9.7 0.1 fusion.14
  9.8 8.6 %gather_fusion = bf16[128,256,128]{2,1,0:T(8,128)(2,1)} fusion(bf16[64,256,128]{2,1,0:T(8,128)(2,1)} %bitcast.64, s32[1024]{0:T(1024)S(1)} %pad_clamp_fusion.1), kind=kCustom, calls=%fused_computation | custom fusion | bytes 16777728 | tf_op jit(solution)/shard_map/jit(_take)/gather | solution.py:80
  18.4 13.4 %convert_select_fusion = f32[128,256,128]{2,1,0:T(8,128)} fusion(bf16[128,256,128]{2,1,0:T(8,128)(2,1)} %gather_fusion, pred[128]{0:T(512)(128)(4,1)S(1)} %compare_and_fusion, pred[128]{0:T(512)(128)(4,1)S(1)} %fusion.14), kind=kLoop, calls=%fused_computation.2 | loop fusion | flops 12582912 | bytes 25166080 | tf_op jit(solution)/shard_map/jit(_where)/select_n | solution.py:79
  31.7 0.0 copy-start
  31.7 0.0 reduce-scatter.2.cloned.1.call-update
  31.8 0.0 all-reduce.6.cloned.1.call-start
  31.8 245.8 %reduce-scatter.2.cloned.1.call-done = f32[4,256,128]{2,1,0:T(8,128)} async-done(((f32[128,256,128]{2,1,0:T(8,128)}), f32[4,256,128]{2,1,0:T(8,128)}) %reduce-scatter.2.cloned.1.call-update) | async-done | bytes 524304 | tf_op jit(solution)/shard_map/reduce_scatter | solution.py:82
  277.7 0.0 copy-done
  277.7 1.9 multiply_reduce_fusion
  279.6 17.0 %psum.42 = f32[4]{0:T(128)S(1)} all-reduce(f32[4]{0:T(128)S(1)} %get-tuple-element.5), channel_id=1, replica_groups=mesh['dp'=32,'own'=8] {'own'}, use_global_device_ids=true, to_apply=%region_6.7 | all-reduce | flops 4 | bytes 32 | tf_op jit(solution)/shard_map/psum | solution.py:85
  296.6 3.3 fusion.7
  299.9 0.0 all-reduce.6.cloned.1.call-update
  299.9 0.0 all-reduce.8.cloned.1.call-start
  300.0 61.9 %all-reduce.6.cloned.1.call-done = f32[4,256,256]{2,1,0:T(8,128)} async-done(((f32[4,256,256]{2,1,0:T(8,128)}), f32[4,256,256]{2,1,0:T(8,128)}) %all-reduce.6.cloned.1.call-update) | async-done | bytes 1048592 | tf_op jit(solution)/shard_map/psum | solution.py:48
  361.9 3.3 fusion.4
  365.2 2.4 convolution_add_fusion.4
  367.6 2.0 fusion.17
  369.5 0.0 all-reduce.8.cloned.1.call-update
  369.6 0.2 all-reduce.10.cloned.1.call-start
  369.8 67.1 %all-reduce.8.cloned.1.call-done = f32[4,256,256]{2,1,0:T(8,128)} async-done(((f32[4,256,256]{2,1,0:T(8,128)}), f32[4,256,256]{2,1,0:T(8,128)}) %all-reduce.8.cloned.1.call-update) | async-done | bytes 1048592 | tf_op jit(solution)/shard_map/psum | solution.py:48
  436.9 3.3 fusion.3
  440.2 1.1 convolution_add_fusion.3
  441.3 2.0 fusion.18
  443.3 0.0 all-reduce.10.cloned.1.call-update
  443.3 0.0 all-reduce.12.cloned.1.call-start
  443.4 67.3 %all-reduce.10.cloned.1.call-done = f32[4,256,256]{2,1,0:T(8,128)} async-done(((f32[4,256,256]{2,1,0:T(8,128)}), f32[4,256,256]{2,1,0:T(8,128)}) %all-reduce.10.cloned.1.call-update) | async-done | bytes 1048592 | tf_op jit(solution)/shard_map/psum | solution.py:48
  510.7 3.3 fusion.2
  514.0 0.0 copy-start.1
  514.0 1.1 convolution_add_fusion.2
  515.1 2.0 fusion.19
  517.0 0.0 copy-start.2
  517.0 0.0 all-reduce.12.cloned.1.call-update
  517.1 0.0 all-reduce.14.cloned.1.call-start
  517.1 67.3 %all-reduce.12.cloned.1.call-done = f32[4,256,256]{2,1,0:T(8,128)} async-done(((f32[4,256,256]{2,1,0:T(8,128)}), f32[4,256,256]{2,1,0:T(8,128)}) %all-reduce.12.cloned.1.call-update) | async-done | bytes 1048592 | tf_op jit(solution)/shard_map/psum | solution.py:48
  584.5 3.3 fusion.1
  587.8 1.1 convolution_add_fusion.1
  588.8 2.0 fusion.20
  590.8 0.0 all-reduce.14.cloned.1.call-update
  590.8 0.3 all-gather.2.cloned.1.call-start
  591.1 67.1 %all-reduce.14.cloned.1.call-done = f32[4,256,256]{2,1,0:T(8,128)} async-done(((f32[4,256,256]{2,1,0:T(8,128)}), f32[4,256,256]{2,1,0:T(8,128)}) %all-reduce.14.cloned.1.call-update) | async-done | bytes 1048592 | tf_op jit(solution)/shard_map/psum | solution.py:48
  658.2 3.3 fusion
  661.5 0.0 copy-done.1
  661.5 2.0 fusion.16
  663.5 0.0 all-gather.2.cloned.1.call-update
  663.5 0.0 copy-done.2
  663.6 98.5 %all-gather.2.cloned.1.call-done = bf16[128,256,128]{2,1,0:T(8,128)(2,1)} async-done(((bf16[4,256,128]{2,1,0:T(8,128)(2,1)}), bf16[128,256,128]{2,1,0:T(8,128)(2,1)}) %all-gather.2.cloned.1.call-update) | async-done | bytes 8388624 | tf_op jit(solution)/shard_map/all_gather | solution.py:96
  762.1 6.5 gather_fusion.1
  768.6 4.6 broadcast_select_fusion
  (6 shorter events, 0.0 us)
Async XLA Ops:
  7.2 270.5 %reduce-scatter.2.cloned.1.call-start = ((), (), s32[]{:S(2)}) async-start(), calls=%async_computation.1 | async-start | bytes 17301504 | tf_op jit(solution)/shard_map/reduce_scatter | solution.py:82
  31.7 245.9 %copy-start = (f32[1,4,256,128]{3,2,1,0:T(8,128)S(1)}, f32[1,4,256,128]{3,2,1,0:T(8,128)}, u32[]{:S(2)}) copy-start(f32[1,4,256,128]{3,2,1,0:T(8,128)} %param.6) | copy-start | bytes 1572868
  31.8 330.1 %all-reduce.6.cloned.1.call-start = ((), (), s32[]{:S(2)}) async-start(), calls=%async_computation.2 | async-start | bytes 2097152 | tf_op jit(solution)/shard_map/psum | solution.py:48
  299.9 137.0 %all-reduce.8.cloned.1.call-start = ((), (), s32[]{:S(2)}) async-start(), calls=%async_computation.3 | async-start | bytes 2097152 | tf_op jit(solution)/shard_map/psum | solution.py:48
  369.6 141.1 %all-reduce.10.cloned.1.call-start = ((), (), s32[]{:S(2)}) async-start(), calls=%async_computation.4 | async-start | bytes 2097152 | tf_op jit(solution)/shard_map/psum | solution.py:48
  443.3 141.2 %all-reduce.12.cloned.1.call-start = ((), (), s32[]{:S(2)}) async-start(), calls=%async_computation.5 | async-start | bytes 2097152 | tf_op jit(solution)/shard_map/psum | solution.py:48
  514.0 147.5 %copy-start.1 = (f32[1,4,256,128]{3,2,1,0:T(8,128)S(1)}, f32[1,4,256,128]{3,2,1,0:T(8,128)}, u32[]{:S(2)}) copy-start(f32[1,4,256,128]{3,2,1,0:T(8,128)} %param.7) | copy-start | bytes 1572868
  517.0 146.5 %copy-start.2 = (s32[64,1]{0,1:T(1,128)S(1)}, s32[64,1]{0,1:T(1,128)}, u32[]{:S(2)}) copy-start(s32[64,1]{0,1:T(1,128)} %param.5) | copy-start | bytes 772
  517.1 141.1 %all-reduce.14.cloned.1.call-start = ((), (), s32[]{:S(2)}) async-start(), calls=%async_computation.6 | async-start | bytes 2097152 | tf_op jit(solution)/shard_map/psum | solution.py:48
  590.8 171.3 %all-gather.2.cloned.1.call-start = ((), (), s32[]{:S(2)}) async-start(), calls=%async_computation.7 | async-start | bytes 8650752 | tf_op jit(solution)/shard_map/all_gather | solution.py:96
Sparse Core Ops, SparseCore 0:
  31.9 245.7 reduce-scatter.1
  300.1 61.7 all-reduce.5
  369.7 67.2 all-reduce.7
  443.4 67.2 all-reduce.9
  517.2 67.2 all-reduce.11
  590.9 67.2 all-reduce.13
  663.6 98.4 all-gather.1
where the time goes:
time: 780 us
  waiting for transfers between devices  675 us (87%)
  matrix products  35.2 us (5%)
  other arithmetic  22.5 us (3%)
  blocking collectives  17 us (2%)
  local copies, waits for them, and re-layouts  15.1 us (2%)
  between operations  14.3 us (2%)
    psum x5, waiting for transfers between devices, gram_total(): return lax.psum(local_gram(values), 'own')  331 us
    reduce_scatter x1, waiting for transfers between devices, on_device(): gradient = lax.psum_scatter(outgoing, 'dp', scatter_dimension=0, tiled=True)  246 us
    all_gather x1, waiting for transfers between devices, on_device(): every_slot = lax.all_gather(weights_low, 'dp', axis=0, tiled=True)  98.5 us
    psum x1, blocking collectives, on_device(): squares = lax.psum(jnp.sum(update * update, axis=(1, 2)), 'own')  17 us
    dot_general x5, matrix products, newton_turn(): jnp.einsum('srt,stu->sru', gram, gram, precision=lax.Precision.HIGHEST, p...  16.5 us
  transfers between devices with their start and end apart: 7, of which 7 were waited for; matrix products, arithmetic and copies ran while one was open for 0% of the time, Pallas kernels for 0%

commit v1 on v0

--- a/solution.py
+++ b/solution.py
@@ -13,6 +13,11 @@
 STEP_SIZE = 0.2
 DECAY = 0.1
 EPSILON = 1e-07
+
+
+def tiled_gather(x, axis, dim):
+    copies = jnp.concatenate([x] * lax.axis_size(axis), axis=dim)
+    return lax.all_to_all(copies, axis, dim, dim, tiled=True)
 
 
 def slot_targets(owner_list, group_count, slot_count):
@@ -93,7 +98,7 @@
     step_factor = STEP_SIZE * 0.2 * math.sqrt(max(block_rows, D))
     master_new = master[0] * (1.0 - STEP_SIZE * DECAY) - step_factor * ortho
     weights_low = master_new.astype(jnp.bfloat16)
-    every_slot = lax.all_gather(weights_low, "dp", axis=0, tiled=True)
+    every_slot = tiled_gather(weights_low, "dp", 0)
     weights = jnp.take(every_slot, target, axis=0)
     return (momentum_new[None], master_new[None], weights)
 

time: 780 us -> 917 us (1.18)
  the two profiles are of different devices: /device:TPU:1 before, /device:TPU:123 now
where the time goes in v1:
time: 917 us; the launch traced here: 916 us
  waiting for transfers between devices  782 us (85%)
  local copies, waits for them, and re-layouts  37.6 us (4%)
  matrix products  35.2 us (4%)
  other arithmetic  22.5 us (2%)
  blocking collectives  14.6 us (2%)
  between operations  14.3 us (2%)
  starting transfers between devices  10.1 us (1%)
    psum x5, waiting for transfers between devices, gram_total(): return lax.psum(local_gram(values), 'own')  336 us
    reduce_scatter x1, waiting for transfers between devices, on_device(): gradient = lax.psum_scatter(outgoing, 'dp', scatter_dimension=0, tiled=True)  242 us
    all_to_all x1, waiting for transfers between devices, tiled_gather(): return lax.all_to_all(copies, axis, dim, dim, tiled=True)  204 us
    unnamed x36, local copies, waits for them, and re-layouts  21.7 us
  transfers between devices with their start and end apart: 7, of which 7 were waited for; matrix products, arithmetic and copies ran while one was open for 0% of the time, Pallas kernels for 0%

profile of v1, /device:TPU:123, one launch (start us, length us, event | category | flops | bytes accessed | tf_op | source)
XLA Modules:
  0.0 916.1 jit_solution(4675048391644902403)
XLA Ops:
  7.2 0.7 fusion.13
  8.0 0.8 select_reduce_fusion.1
  8.9 0.7 multiply_add_fusion.1
  9.8 8.6 gather_fusion
  18.4 13.4 %convert_select_fusion = f32[128,256,128]{2,1,0:T(8,128)} fusion(bf16[128,256,128]{2,1,0:T(8,128)(2,1)} %gather_fusion, pred[128]{0:T(512)(128)(4,1)S(1)} %compare_and_fusion, pred[128]{0:T(512)(128)(4,1)S(1)} %fusion.14), kind=kLoop, calls=%fused_computation.2 | loop fusion | flops 12582912 | bytes 25166080 | tf_op jit(solution)/shard_map/jit(_where)/select_n | solution.py:84
  31.8 242.0 %reduce-scatter.2.cloned.1.call-done = f32[4,256,128]{2,1,0:T(8,128)} async-done(((f32[128,256,128]{2,1,0:T(8,128)}), f32[4,256,128]{2,1,0:T(8,128)}) %reduce-scatter.2.cloned.1.call-update) | async-done | bytes 524304 | tf_op jit(solution)/shard_map/reduce_scatter | solution.py:87
  273.8 1.9 multiply_reduce_fusion
  275.7 14.6 %psum.42 = f32[4]{0:T(128)S(1)} all-reduce(f32[4]{0:T(128)S(1)} %get-tuple-element.7), channel_id=1, replica_groups=mesh['dp'=32,'own'=8] {'own'}, use_global_device_ids=true, to_apply=%region_6.7 | all-reduce | flops 4 | bytes 32 | tf_op jit(solution)/shard_map/psum | solution.py:90
  290.4 3.3 fusion.7
  293.8 66.8 %all-reduce.6.cloned.1.call-done = f32[4,256,256]{2,1,0:T(8,128)} async-done(((f32[4,256,256]{2,1,0:T(8,128)}), f32[4,256,256]{2,1,0:T(8,128)}) %all-reduce.6.cloned.1.call-update) | async-done | bytes 1048592 | tf_op jit(solution)/shard_map/psum | solution.py:53
  360.5 3.3 fusion.4
  363.8 2.4 convolution_add_fusion.4
  366.2 2.0 fusion.16
  368.4 67.1 %all-reduce.8.cloned.1.call-done = f32[4,256,256]{2,1,0:T(8,128)} async-done(((f32[4,256,256]{2,1,0:T(8,128)}), f32[4,256,256]{2,1,0:T(8,128)}) %all-reduce.8.cloned.1.call-update) | async-done | bytes 1048592 | tf_op jit(solution)/shard_map/psum | solution.py:53
  435.6 3.3 fusion.3
  438.9 1.1 convolution_add_fusion.3
  440.0 2.0 fusion.17
  442.0 67.3 %all-reduce.10.cloned.1.call-done = f32[4,256,256]{2,1,0:T(8,128)} async-done(((f32[4,256,256]{2,1,0:T(8,128)}), f32[4,256,256]{2,1,0:T(8,128)}) %all-reduce.10.cloned.1.call-update) | async-done | bytes 1048592 | tf_op jit(solution)/shard_map/psum | solution.py:53
  509.3 3.3 fusion.2
  512.7 1.1 convolution_add_fusion.2
  513.7 2.0 fusion.18
  515.7 0.3 all-reduce.14.cloned.1.call-start
  516.0 67.1 %all-reduce.12.cloned.1.call-done = f32[4,256,256]{2,1,0:T(8,128)} async-done(((f32[4,256,256]{2,1,0:T(8,128)}), f32[4,256,256]{2,1,0:T(8,128)}) %all-reduce.12.cloned.1.call-update) | async-done | bytes 1048592 | tf_op jit(solution)/shard_map/psum | solution.py:53
  583.1 3.3 fusion.1
  586.4 1.1 convolution_add_fusion.1
  587.5 2.0 fusion.19
  589.5 67.4 %all-reduce.14.cloned.1.call-done = f32[4,256,256]{2,1,0:T(8,128)} async-done(((f32[4,256,256]{2,1,0:T(8,128)}), f32[4,256,256]{2,1,0:T(8,128)}) %all-reduce.14.cloned.1.call-update) | async-done | bytes 1048592 | tf_op jit(solution)/shard_map/psum | solution.py:53
  656.9 3.3 fusion
  660.2 2.0 constant_dynamic-update-slice_fusion.31
  662.2 0.7 constant_dynamic-update-slice_fusion.30
  662.9 0.7 constant_dynamic-update-slice_fusion.29
  663.6 0.7 constant_dynamic-update-slice_fusion.28
  664.4 0.7 constant_dynamic-update-slice_fusion.27
  665.1 0.7 constant_dynamic-update-slice_fusion.26
  665.8 0.7 constant_dynamic-update-slice_fusion.25
  666.6 0.7 constant_dynamic-update-slice_fusion.24
  667.3 0.7 constant_dynamic-update-slice_fusion.23
  668.0 0.7 constant_dynamic-update-slice_fusion.22
  668.8 0.7 constant_dynamic-update-slice_fusion.21
  669.5 0.7 constant_dynamic-update-slice_fusion.20
  670.2 0.7 constant_dynamic-update-slice_fusion.19
  670.9 0.7 constant_dynamic-update-slice_fusion.18
  671.6 0.7 constant_dynamic-update-slice_fusion.17
  672.3 0.7 constant_dynamic-update-slice_fusion.16
  673.1 0.7 constant_dynamic-update-slice_fusion.15
  673.8 0.7 constant_dynamic-update-slice_fusion.14
  674.5 0.7 constant_dynamic-update-slice_fusion.13
  675.3 0.7 constant_dynamic-update-slice_fusion.12
  676.0 0.7 constant_dynamic-update-slice_fusion.11
  676.7 0.7 constant_dynamic-update-slice_fusion.10
  677.4 0.7 constant_dynamic-update-slice_fusion.9
  678.1 0.7 constant_dynamic-update-slice_fusion.8
  678.8 0.7 constant_dynamic-update-slice_fusion.7
  679.6 0.7 constant_dynamic-update-slice_fusion.6
  680.3 0.7 constant_dynamic-update-slice_fusion.5
  681.0 0.7 constant_dynamic-update-slice_fusion.4
  681.7 0.7 constant_dynamic-update-slice_fusion.3
  682.5 0.7 constant_dynamic-update-slice_fusion.2
  683.2 0.7 constant_dynamic-update-slice_fusion.1
  683.9 0.7 constant_dynamic-update-slice_fusion
  684.6 9.5 %all-to-all-start = ((bf16[128,256,128]{2,1,0:T(8,128)(2,1)}), bf16[128,256,128]{2,1,0:T(8,128)(2,1)}, u32[]{:S(2)}, u32[]{:S(2)}) async-start(bf16[128,256,128]{2,1,0:T(8,128)(2,1)} %constant_dynamic-update-slice_fusion), calls=%async_computation.1 | async-start | bytes 16777216 | tf_op jit(solution)/shard_map/all_to_all | solution.py:20
  694.2 203.9 %all-to-all-done = bf16[128,256,128]{2,1,0:T(8,128)(2,1)} async-done(((bf16[128,256,128]{2,1,0:T(8,128)(2,1)}), bf16[128,256,128]{2,1,0:T(8,128)(2,1)}, u32[]{:S(2)}, u32[]{:S(2)}) %all-to-all-start) | async-done | bytes 8388640 | tf_op jit(solution)/shard_map/all_to_all | solution.py:20
  898.1 6.5 gather_fusion.1
  904.6 4.6 broadcast_select_fusion
  (26 shorter events, 0.8 us)
Async XLA Ops:
  7.2 266.6 %reduce-scatter.2.cloned.1.call-start = ((), (), s32[]{:S(2)}) async-start(), calls=%async_computation.2 | async-start | bytes 17301504 | tf_op jit(solution)/shard_map/reduce_scatter | solution.py:87
  31.7 242.1 %copy-start = (f32[1,4,256,128]{3,2,1,0:T(8,128)S(1)}, f32[1,4,256,128]{3,2,1,0:T(8,128)}, u32[]{:S(2)}) copy-start(f32[1,4,256,128]{3,2,1,0:T(8,128)} %param.6) | copy-start | bytes 1572868
  31.8 328.8 %all-reduce.6.cloned.1.call-start = ((), (), s32[]{:S(2)}) async-start(), calls=%async_computation.3 | async-start | bytes 2097152 | tf_op jit(solution)/shard_map/psum | solution.py:53
  293.7 141.8 %all-reduce.8.cloned.1.call-start = ((), (), s32[]{:S(2)}) async-start(), calls=%async_computation.4 | async-start | bytes 2097152 | tf_op jit(solution)/shard_map/psum | solution.py:53
  368.2 141.1 %all-reduce.10.cloned.1.call-start = ((), (), s32[]{:S(2)}) async-start(), calls=%async_computation.5 | async-start | bytes 2097152 | tf_op jit(solution)/shard_map/psum | solution.py:53
  442.0 141.1 %all-reduce.12.cloned.1.call-start = ((), (), s32[]{:S(2)}) async-start(), calls=%async_computation.6 | async-start | bytes 2097152 | tf_op jit(solution)/shard_map/psum | solution.py:53
  512.6 147.5 %copy-start.1 = (f32[1,4,256,128]{3,2,1,0:T(8,128)S(1)}, f32[1,4,256,128]{3,2,1,0:T(8,128)}, u32[]{:S(2)}) copy-start(f32[1,4,256,128]{3,2,1,0:T(8,128)} %param.7) | copy-start | bytes 1572868
  515.7 141.1 %all-reduce.14.cloned.1.call-start = ((), (), s32[]{:S(2)}) async-start(), calls=%async_computation.7 | async-start | bytes 2097152 | tf_op jit(solution)/shard_map/psum | solution.py:53
  684.6 9.5 %copy-start.2 = (s32[64,1]{0,1:T(1,128)S(1)}, s32[64,1]{0,1:T(1,128)}, u32[]{:S(2)}) copy-start(s32[64,1]{0,1:T(1,128)} %param.5) | copy-start | bytes 772
  684.6 213.5 %all-to-all-start = ((bf16[128,256,128]{2,1,0:T(8,128)(2,1)}), bf16[128,256,128]{2,1,0:T(8,128)(2,1)}, u32[]{:S(2)}, u32[]{:S(2)}) async-start(bf16[128,256,128]{2,1,0:T(8,128)(2,1)} %constant_dynamic-update-slice_fusion), calls=%async_computation.1 | async-start | bytes 16777216 | tf_op jit(solution)/shard_map/all_to_all | solution.py:20
Sparse Core Ops, SparseCore 0:
  31.9 241.8 reduce-scatter.1
  293.9 66.6 all-reduce.5
  368.3 67.2 all-reduce.7
  442.1 67.2 all-reduce.9
  515.8 67.2 all-reduce.11
  589.6 67.2 all-reduce.13
